TPU v7x, 32 devices: a whole 2x2x4 slice. The times are simulated.
32 devices in a mesh: section: 4 (over x, core), sp: 2 (over y), rep: 4 (over z).
Axes of the slice: x: 2, y: 2, z: 4, core: 2. Of those that a mesh axis runs over, the one named last changes fastest.
Arguments:
- tokens: float32 [2, 2, 24, 3072], P('sp', None, 'section', 'rep'), may hold values from -120 to 120
- mod_scale: float32 [3072], replicated, may hold values from -3 to 3
- mod_shift: float32 [3072], replicated, may hold values from -3 to 3
- proj_weight: float32 [64, 3072], replicated, may hold values from -0.109375 to 0.109375
- proj_bias: float32 [64], replicated, may hold values from -3 to 3
- noisy_latent: float32 [2, 4, 48, 16], P(None, 'sp', 'section'), may hold values from -120 to 120
- in_weight: float32 [3, 3, 3, 16, 512], replicated, may hold values from -0.3125 to 0.3125
- in_bias: float32 [512], replicated, may hold values from -3 to 3
- conv_weight: bfloat16 [3, 3, 3, 256, 512], P(None, None, None, 'rep'), may hold values from -0.0546875 to 0.0546875
- conv_bias: float32 [256], P('rep'), may hold values from -3 to 3
- norm_gain: float32 [256], P('rep'), may hold values from 0.25 to 1.75
- norm_bias: float32 [256], P('rep'), may hold values from -3 to 3
Outputs:
- decoded: float32 [8, 96, 512], P('sp', 'section', 'rep')
All inputs are finite; a program needn't handle non-finite values.
Results may differ from a plain program's by a relative error of at most 0.0026.
Values sent between devices are 32-bit elements; how exact they have to be, the bound alone decides.
No kernel may reach another device: no remote copies, remote signals or barrier semaphores. Data moves between devices by JAX's collectives and lax.ppermute only.
A program may use at most 64 MiB of HBM per device.

v0:
```python
import jax
import jax.numpy as jnp
from jax import lax
from jax.sharding import PartitionSpec as P

D = 3072
LC = 16
CO = 256
GROUPS = 32


def with_halo(block, sides, width):
    for axis, dim in sides:
        count = lax.axis_size(axis)
        forward = [(i, i + 1) for i in range(count - 1)]
        backward = [(target, source) for source, target in forward]
        low = lax.ppermute(
            lax.slice_in_dim(block, block.shape[dim] - width, None, axis=dim), axis, forward
        )
        high = lax.ppermute(lax.slice_in_dim(block, 0, width, axis=dim), axis, backward)
        block = jnp.concatenate([low, block, high], axis=dim)
    return block


def valid_conv(volume, kernel, kernel_spec, precision_mode):
    front = jnp.concatenate([volume[:1], volume[:1], volume], axis=0)
    result = lax.conv_general_dilated(
        front[None],
        kernel,
        (1, 1, 1),
        "VALID",
        dimension_numbers=("NDHWC", kernel_spec, "NDHWC"),
        precision=precision_mode,
        preferred_element_type=jnp.float32,
    )
    return result[0]


def per_device(
    tokens,
    mod_scale,
    mod_shift,
    proj_weight,
    proj_bias,
    noisy_latent,
    in_weight,
    in_bias,
    conv_weight,
    conv_bias,
    norm_gain,
    norm_bias,
):
    local_width = tokens.shape[-1]
    scaled_weight = proj_weight * (1.0 + mod_scale)[None, :]
    center_column = jnp.sum(scaled_weight, axis=1)
    shift_column = (
        jnp.dot(
            proj_weight,
            mod_shift,
            precision=lax.Precision.HIGHEST,
            preferred_element_type=jnp.float32,
        )
        + proj_bias
    )
    local_weight = lax.dynamic_slice_in_dim(
        scaled_weight, lax.axis_index("rep") * local_width, local_width, 1
    )
    moved_tokens = lax.all_to_all(tokens, "sp", split_axis=1, concat_axis=0, tiled=True)
    projected = lax.dot_general(
        moved_tokens,
        local_weight,
        (((3,), (1,)), ((), ())),
        precision=lax.Precision.HIGHEST,
        preferred_element_type=jnp.float32,
    )
    projected, first_sums, square_sums = (
        projected,
        jnp.sum(moved_tokens, axis=-1),
        jnp.sum(moved_tokens * moved_tokens, axis=-1),
    )
    projected, first_sums, square_sums = lax.psum((projected, first_sums, square_sums), "rep")
    token_mean = first_sums / D
    token_var = square_sums / D - token_mean * token_mean
    velocity = (
        lax.rsqrt(token_var + 1e-06)[..., None]
        * (projected - token_mean[..., None] * center_column)
        + shift_column
    )
    frames, slab_rows, band_cols = (velocity.shape[0], velocity.shape[1], velocity.shape[2])
    patches = (
        velocity.reshape(frames, slab_rows, band_cols, LC, 2, 2)
        .transpose(0, 1, 4, 2, 5, 3)
        .reshape(frames, 2 * slab_rows, 2 * band_cols, LC)
    )
    clean = noisy_latent - 0.5 * patches
    extended = with_halo(clean, (("section", 2), ("sp", 1)), 2)
    inner_features = valid_conv(extended, in_weight, "DHWIO", lax.Precision.HIGHEST) + in_bias
    latent_rows = 2 * slab_rows
    latent_cols = 2 * band_cols
    row_global = lax.axis_index("sp") * latent_rows - 1 + jnp.arange(latent_rows + 2)
    col_global = lax.axis_index("section") * latent_cols - 1 + jnp.arange(latent_cols + 2)
    row_inside = (row_global >= 0) & (row_global < latent_rows * lax.axis_size("sp"))
    col_inside = (col_global >= 0) & (col_global < latent_cols * lax.axis_size("section"))
    inside = row_inside[None, :, None, None] & col_inside[None, None, :, None]
    features = jnp.where(inside, inner_features, 0.0).astype(jnp.bfloat16)
    upsampled = jnp.repeat(jnp.repeat(features, 2, axis=1), 2, axis=2)[:, 1:-1, 1:-1, :]
    mixed = valid_conv(upsampled, conv_weight, "DHWOI", None) + conv_bias
    group_size = CO // GROUPS
    local_groups = mixed.shape[-1] // group_size
    grouped = mixed.reshape(-1, local_groups, group_size)
    cell_count = grouped.shape[0] * group_size * lax.axis_size("section") * lax.axis_size("sp")
    group_mean = lax.psum(jnp.sum(grouped, axis=(0, 2)), ("section", "sp")) / cell_count
    deviation = grouped - group_mean[None, :, None]
    group_var = (
        lax.psum(jnp.sum(deviation * deviation, axis=(0, 2)), ("section", "sp")) / cell_count
    )
    normed = (
        (grouped - group_mean[None, :, None]) * lax.rsqrt(group_var + 1e-06)[None, :, None]
    ).reshape(mixed.shape)
    activated = jax.nn.silu(normed * norm_gain + norm_bias)
    out_rows, out_cols, out_chan = (activated.shape[1], activated.shape[2], activated.shape[3])
    return activated.transpose(1, 2, 3, 0).reshape(out_rows, out_cols, out_chan * frames)


def solution(mesh):
    return jax.shard_map(
        per_device,
        mesh=mesh,
        in_specs=(
            P("sp", None, "section", "rep"),
            P(),
            P(),
            P(),
            P(),
            P(None, "sp", "section", None),
            P(),
            P(),
            P(None, None, None, "rep", None),
            P("rep"),
            P("rep"),
            P("rep"),
        ),
        out_specs=P("sp", "section", "rep"),
        check_vma=False,
    )
```

profile of v0, /device:TPU:0, one launch (start us, length us, event | category | flops | bytes accessed | tf_op | source)
XLA Modules:
  0.0 79.5 jit_solution(5452324065720546734)
XLA Ops:
  0.0 0.0 copy-start
  0.0 0.0 copy-start.2
  0.0 1.6 %copy.53 = f32[1,2,6,768]{3,0,2,1:T(1,128)} copy(f32[1,2,6,768]{3,1,2,0:T(2,128)} %param.12) | data formatting | bytes 73728 | tf_op args[0]
  1.6 4.2 %all-to-all-start = ((f32[1,2,6,768]{3,0,2,1:T(1,128)}), f32[1,2,6,768]{3,0,2,1:T(1,128)S(1)}, u32[]{:S(2)}, u32[]{:S(2)}) async-start(f32[1,2,6,768]{3,0,2,1:T(1,128)} %copy.53), calls=%async_computation | async-start | bytes 73728 | tf_op jit(solution)/shard_map/all_to_all | solution.py:68
  5.8 0.7 broadcast_add_fusion
  6.5 1.3 %fusion.37 = (f32[64]{0:T(128)S(1)}, f32[64,3072]{1,0:T(8,128)S(1)}) fusion(f32[64,3072]{1,0:T(8,128)} %param.15, f32[3072]{0:T(1024)S(1)} %broadcast_add_fusion), kind=kLoop, calls=%fused_computation.63 | loop fusion | flops 393152 | bytes 1585408 | tf_op jit(solution)/shard_map/reduce_sum | solution.py:55
  7.9 0.0 copy-start.10
  7.9 0.0 copy-done.1
  7.9 0.0 copy-done.6
  7.9 0.0 copy-done.3
  7.9 0.7 fusion.11
  8.7 1.1 %all-to-all-done = f32[1,2,6,768]{3,0,2,1:T(1,128)S(1)} async-done(((f32[1,2,6,768]{3,0,2,1:T(1,128)}), f32[1,2,6,768]{3,0,2,1:T(1,128)S(1)}, u32[]{:S(2)}, u32[]{:S(2)}) %all-to-all-start) | async-done | bytes 36896 | tf_op jit(solution)/shard_map/all_to_all | solution.py:68
  9.8 0.2 convolution_bitcast_fusion
  10.1 0.2 multiply_reduce_fusion
  10.3 19.4 %all-reduce = (f32[2,1,6,64]{3,2,0,1:T(8,128)S(1)}, f32[2,1,6]{2,0,1:T(2,128)S(1)}, f32[2,1,6]{2,0,1:T(2,128)S(1)}) all-reduce(f32[2,1,6,64]{3,2,0,1:T(8,128)S(1)} %convolution_bitcast_fusion, f32[2,1,6]{2,0,1:T(2,128)S(1)} %bitcast.85, f32[2,1,6]{2,0,1:T(2,128)S(1)} %bitcast.84), channel_id=1, replica_groups=mesh['section'=4,'sp'=2,'rep'=4] {'rep'}, use_global_device_ids=true, to_apply=%region_4.0 | all-reduce | flops 792 | bytes 6336 | tf_op jit(solution)/shard_map/psum | solution.py:81
  29.7 0.1 add_multiply_fusion
  29.8 0.1 copy.56
  29.9 0.1 copy.57
  30.0 0.0 copy-done.2
  30.1 1.3 %collective-permute-start = (f32[2,2,2,16]{3,1,2,0:T(2,128)S(1)}, f32[2,2,2,16]{3,1,2,0:T(2,128)S(1)}, u32[]{:S(2)}, u32[]{:S(2)}) collective-permute-start(f32[2,2,2,16]{3,1,2,0:T(2,128)S(1)} %get-tuple-element.12), channel_id=1, source_target_pairs={{0,8},{8,16},{16,24},{1,9},{9,17},{17,25},{2,10},{10,18},{18,26},{... | collective-permute-start | bytes 1544 | tf_op jit(solution)/shard_map/ppermute | solution.py:17
  31.4 1.3 %collective-permute-start.1 = (f32[2,2,2,16]{3,1,2,0:T(2,128)S(1)}, f32[2,2,2,16]{3,1,2,0:T(2,128)S(1)}, u32[]{:S(2)}, u32[]{:S(2)}) collective-permute-start(f32[2,2,2,16]{3,1,2,0:T(2,128)S(1)} %get-tuple-element.13), channel_id=1, source_target_pairs={{8,0},{16,8},{24,16},{9,1},{17,9},{25,17},{10,2},{18,10},{26,18},{... | collective-permute-start | bytes 1544 | tf_op jit(solution)/shard_map/ppermute | solution.py:20
  32.7 0.0 collective-permute-done
  32.7 3.5 %collective-permute-done.1 = f32[2,2,2,16]{3,1,2,0:T(2,128)S(1)} collective-permute-done((f32[2,2,2,16]{3,1,2,0:T(2,128)S(1)}, f32[2,2,2,16]{3,1,2,0:T(2,128)S(1)}, u32[]{:S(2)}, u32[]{:S(2)}) %collective-permute-start.1) | collective-permute-done | bytes 544 | tf_op jit(solution)/shard_map/ppermute | solution.py:20
  36.2 1.3 %collective-permute-start.3 = (f32[2,2,16,16]{3,1,2,0:T(2,128)S(1)}, f32[2,2,16,16]{3,1,2,0:T(2,128)S(1)}, u32[]{:S(2)}, u32[]{:S(2)}) collective-permute-start(f32[2,2,16,16]{3,1,2,0:T(2,128)S(1)} %pad_maximum_fusion.4), channel_id=1, source_target_pairs={{4,0},{5,1},{6,2},{7,3},{12,8},{13,9},{14,10},{15,11},{20,16},{21,... | collective-permute-start | bytes 12296 | tf_op jit(solution)/shard_map/ppermute | solution.py:20
  37.5 4.5 %collective-permute-start.2 = (f32[2,2,16,16]{3,1,2,0:T(2,128)S(1)}, f32[2,2,16,16]{3,1,2,0:T(2,128)S(1)}, u32[]{:S(2)}, u32[]{:S(2)}) collective-permute-start(f32[2,2,16,16]{3,1,2,0:T(2,128)S(1)} %pad_maximum_fusion.4), channel_id=1, source_target_pairs={{0,4},{1,5},{2,6},{3,7},{8,12},{9,13},{10,14},{11,15},{16,20},{17,... | collective-permute-start | bytes 12296 | tf_op jit(solution)/shard_map/ppermute | solution.py:17
  42.1 0.1 broadcast_and_fusion
  42.1 0.0 collective-permute-done.3
  42.1 1.5 %collective-permute-done.2 = f32[2,2,16,16]{3,1,2,0:T(2,128)S(1)} collective-permute-done((f32[2,2,16,16]{3,1,2,0:T(2,128)S(1)}, f32[2,2,16,16]{3,1,2,0:T(2,128)S(1)}, u32[]{:S(2)}, u32[]{:S(2)}) %collective-permute-start.2) | collective-permute-done | bytes 4128 | tf_op jit(solution)/shard_map/ppermute | solution.py:17
  43.7 0.1 maximum_maximum_fusion
  43.8 0.0 copy-start.4
  43.9 2.8 %convolution_select_fusion = f32[2,4,8,2,512]{4,2,3,1,0:T(8,128)S(1)} fusion(f32[3,3,3,16,512]{4,3,2,1,0:T(8,128)} %param.18, f32[4,6,1,7,2,16]{5,3,4,1,0,2:T(8,128)S(1)} %slice.29, f32[4,6,1,8,2,16]{5,3,4,1,0,2:T(8,128)S(1)} %copy.60, pred[8,2]{0,1:T(4,128)(4,1)S(1)} %copy-done.10), kind=kOutput, calls=%fused_computation.8 | convolution fusion | flops 339841024 | bytes 1192976 | tf_op jit(solution)/shard_map/conv_general_dilated | solution.py:27
  46.7 0.2 copy.61
  46.9 0.1 fusion.19
  47.0 0.1 broadcast_in_dim.23
  47.1 0.1 reshape.129
  47.3 0.1 slice.31
  47.3 0.1 slice.32
  47.4 0.2 maximum_bitcast_fusion
  47.6 0.5 copy.68
  48.1 0.0 copy-start.5
  48.1 0.0 copy-start.9
  48.2 0.3 pad.1.clone
  48.4 0.4 copy.64
  48.9 0.1 slice.33
  49.0 0.0 copy-done
  49.0 0.0 copy-done.5
  49.0 0.0 copy-done.9
  49.0 0.0 copy-start.7
  49.0 0.0 copy-start.8
  49.0 2.0 %select_reduce_fusion.1 = (f32[64]{0:T(128)S(1)}, f32[2,4,8,4,64]{4,2,3,1,0:T(8,128)S(1)}) fusion(f32[64]{0:T(128)S(1)} %copy-done.5, pred[8,4]{0,1:T(4,128)(4,1)S(1)} %copy-done.9, bf16[3,3,3,64,512]{4,3,2,1,0:T(8,128)(2,1)S(1)} %copy-done, bf16[4,6,1,7,2,512]{5,3,4,1,0,2:T(8,128)(2,1)S(1)} %slice.33, bf16[4,6,1,8,4,512]{5,3,4,1,0,2:T(8,128)(2,1)S(1)} %copy.64), kind=kOutput, calls=%fused_computation.31 | convolution fusion | flops 456589248 | bytes 2966048 | tf_op jit(solution)/shard_map/conv_general_dilated | solution.py:27
  51.0 0.1 reduce_sum.69
  51.1 0.1 reduce_sum.70
  51.2 14.4 %psum.38 = f32[8]{0:T(128)S(1)} all-reduce(f32[8]{0:T(128)S(1)} %reduce_sum.70), channel_id=1, replica_groups=mesh['section'=4,'sp'=2,'rep'=4] {'section','sp'}, use_global_device_ids=true, to_apply=%region_8.9 | all-reduce | flops 8 | bytes 64 | tf_op jit(solution)/shard_map/psum | solution.py:112
  65.7 0.1 sub.42
  65.7 0.1 sub.43
  65.8 0.1 select_reduce_fusion
  65.9 0.1 reduce_sum.72
  66.0 0.1 reduce_sum.73
  66.2 12.2 %psum.39 = f32[8]{0:T(128)S(1)} all-reduce(f32[8]{0:T(128)S(1)} %reduce_sum.73), channel_id=1, replica_groups=mesh['section'=4,'sp'=2,'rep'=4] {'section','sp'}, use_global_device_ids=true, to_apply=%region_11.12 | all-reduce | flops 8 | bytes 64 | tf_op jit(solution)/shard_map/psum | solution.py:115
  78.4 0.1 mul.129
  78.5 0.1 mul.130
  78.6 0.1 multiply_bitcast_fusion
  78.7 0.2 copy.66
  78.8 0.7 copy.67
  (22 shorter events, 0.3 us)
Async XLA Ops:
  0.0 49.0 %copy-start = (bf16[3,3,3,64,512]{4,3,2,1,0:T(8,128)(2,1)S(1)}, bf16[3,3,3,64,512]{4,3,2,1,0:T(8,128)(2,1)}, u32[]{:S(2)}) copy-start(bf16[3,3,3,64,512]{4,3,2,1,0:T(8,128)(2,1)} %param.20) | copy-start | bytes 5308420
  0.0 7.9 %copy-start.1 = (f32[64,3072]{1,0:T(8,128)S(1)}, f32[64,3072]{1,0:T(8,128)}, u32[]{:S(2)}) copy-start(f32[64,3072]{1,0:T(8,128)} %param.15) | copy-start | bytes 2359300
  0.0 7.9 %copy-start.6 = (f32[64]{0:T(128)S(1)}, f32[64]{0:T(128)}, u32[]{:S(2)}) copy-start(f32[64]{0:T(128)} %param.16) | copy-start | bytes 772
  0.0 7.9 %copy-start.3 = (f32[3072]{0:T(1024)S(1)}, f32[3072]{0:T(1024)}, u32[]{:S(2)}) copy-start(f32[3072]{0:T(1024)} %param.14) | copy-start | bytes 36868
  0.0 30.0 %copy-start.2 = (f32[2,2,12,16]{3,1,2,0:T(2,128)S(1)}, f32[2,2,12,16]{3,1,2,0:T(2,128)}, u32[]{:S(2)}) copy-start(f32[2,2,12,16]{3,1,2,0:T(2,128)} %param.17) | copy-start | bytes 9220
  1.6 8.2 %all-to-all-start = ((f32[1,2,6,768]{3,0,2,1:T(1,128)}), f32[1,2,6,768]{3,0,2,1:T(1,128)S(1)}, u32[]{:S(2)}, u32[]{:S(2)}) async-start(f32[1,2,6,768]{3,0,2,1:T(1,128)} %copy.53), calls=%async_computation | async-start | bytes 73728 | tf_op jit(solution)/shard_map/all_to_all | solution.py:68
  7.9 36.0 %copy-start.10 = (pred[8,2]{0,1:T(4,128)(4,1)S(1)}, pred[8,2]{0,1:T(4,128)(4,1)}, u32[]{:S(2)}) copy-start(pred[8,2]{0,1:T(4,128)(4,1)} %constant.62) | copy-start | bytes 52
  30.1 2.6 %collective-permute-start = (f32[2,2,2,16]{3,1,2,0:T(2,128)S(1)}, f32[2,2,2,16]{3,1,2,0:T(2,128)S(1)}, u32[]{:S(2)}, u32[]{:S(2)}) collective-permute-start(f32[2,2,2,16]{3,1,2,0:T(2,128)S(1)} %get-tuple-element.12), channel_id=1, source_target_pairs={{0,8},{8,16},{16,24},{1,9},{9,17},{17,25},{2,10},{10,18},{18,26},{... | collective-permute-start | bytes 1544 | tf_op jit(solution)/shard_map/ppermute | solution.py:17
  31.4 4.8 %collective-permute-start.1 = (f32[2,2,2,16]{3,1,2,0:T(2,128)S(1)}, f32[2,2,2,16]{3,1,2,0:T(2,128)S(1)}, u32[]{:S(2)}, u32[]{:S(2)}) collective-permute-start(f32[2,2,2,16]{3,1,2,0:T(2,128)S(1)} %get-tuple-element.13), channel_id=1, source_target_pairs={{8,0},{16,8},{24,16},{9,1},{17,9},{25,17},{10,2},{18,10},{26,18},{... | collective-permute-start | bytes 1544 | tf_op jit(solution)/shard_map/ppermute | solution.py:20
  36.2 5.9 %collective-permute-start.3 = (f32[2,2,16,16]{3,1,2,0:T(2,128)S(1)}, f32[2,2,16,16]{3,1,2,0:T(2,128)S(1)}, u32[]{:S(2)}, u32[]{:S(2)}) collective-permute-start(f32[2,2,16,16]{3,1,2,0:T(2,128)S(1)} %pad_maximum_fusion.4), channel_id=1, source_target_pairs={{4,0},{5,1},{6,2},{7,3},{12,8},{13,9},{14,10},{15,11},{20,16},{21,... | collective-permute-start | bytes 12296 | tf_op jit(solution)/shard_map/ppermute | solution.py:20
  37.5 6.1 %collective-permute-start.2 = (f32[2,2,16,16]{3,1,2,0:T(2,128)S(1)}, f32[2,2,16,16]{3,1,2,0:T(2,128)S(1)}, u32[]{:S(2)}, u32[]{:S(2)}) collective-permute-start(f32[2,2,16,16]{3,1,2,0:T(2,128)S(1)} %pad_maximum_fusion.4), channel_id=1, source_target_pairs={{0,4},{1,5},{2,6},{3,7},{8,12},{9,13},{10,14},{11,15},{16,20},{17,... | collective-permute-start | bytes 12296 | tf_op jit(solution)/shard_map/ppermute | solution.py:17
  43.8 3.0 %copy-start.4 = (f32[512]{0:T(512)S(1)}, f32[512]{0:T(512)}, u32[]{:S(2)}) copy-start(f32[512]{0:T(512)} %param.19) | copy-start | bytes 6148
  48.1 0.9 %copy-start.5 = (f32[64]{0:T(128)S(1)}, f32[64]{0:T(128)}, u32[]{:S(2)}) copy-start(f32[64]{0:T(128)} %param.21) | copy-start | bytes 772
  48.1 0.9 %copy-start.9 = (pred[8,4]{0,1:T(4,128)(4,1)S(1)}, pred[8,4]{0,1:T(4,128)(4,1)}, u32[]{:S(2)}) copy-start(pred[8,4]{0,1:T(4,128)(4,1)} %constant.61) | copy-start | bytes 100
  49.0 29.6 %copy-start.7 = (f32[64]{0:T(128)S(1)}, f32[64]{0:T(128)}, u32[]{:S(2)}) copy-start(f32[64]{0:T(128)} %param.23) | copy-start | bytes 772
  49.0 29.6 %copy-start.8 = (f32[64]{0:T(128)S(1)}, f32[64]{0:T(128)}, u32[]{:S(2)}) copy-start(f32[64]{0:T(128)} %param.22) | copy-start | bytes 772
where the time goes:
time: 80 us; the launch traced here: 79.5 us
  blocking collectives  46.1 us (58%)
  starting transfers between devices  12.7 us (16%)
  waiting for transfers between devices  6.12 us (8%)
  matrix products  5.79 us (7%)
  local copies, waits for them, and re-layouts  5.24 us (7%)
  other arithmetic  3.28 us (4%)
    psum x1, blocking collectives, per_device(): lax.psum((projected, first_sums, square_sums), 'rep')  19.4 us
    psum x1, blocking collectives, per_device(): lax.psum(jnp.sum(grouped, axis=(0, 2)), ('section', 'sp')) / cell_count  14.4 us
    psum x1, blocking collectives, per_device(): lax.psum(jnp.sum(deviation * deviation, axis=(0, 2)), ('section', 'sp'))  12.2 us
    ppermute x2, starting transfers between devices, with_halo(): lax.ppermute(lax.slice_in_dim(block, block.shape[dim] - width, None, axis...  5.84 us
    conv_general_dilated x2, matrix products, valid_conv(): lax.conv_general_dilated(front[None], kernel, (1, 1, 1), 'VALID', dimensi...  4.83 us
    all_to_all x1, starting transfers between devices, per_device(): lax.all_to_all(tokens, 'sp', split_axis=1, concat_axis=0, tiled=True)  4.24 us
    ppermute x2, waiting for transfers between devices, with_halo(): lax.ppermute(lax.slice_in_dim(block, 0, width, axis=dim), axis, backward)  3.47 us
    ppermute x2, starting transfers between devices, with_halo(): lax.ppermute(lax.slice_in_dim(block, 0, width, axis=dim), axis, backward)  2.58 us
  transfers between devices with their start and end apart: 5, of which 3 were waited for; matrix products, arithmetic and copies ran while one was open for 4% of the time, Pallas kernels for 0%

commit v1 on v0

--- a/solution.py
+++ b/solution.py
@@ -7,6 +7,12 @@
 LC = 16
 CO = 256
 GROUPS = 32
+
+
+def exchange_blocks(block, mesh_axis, split, join):
+    pieces = jnp.split(block, lax.axis_size(mesh_axis), axis=split)
+    incoming = lax.all_to_all(jnp.stack(pieces), mesh_axis, 0, 0)
+    return jnp.concatenate(incoming, axis=join)
 
 
 def with_halo(block, sides, width):
@@ -65,7 +71,7 @@
     local_weight = lax.dynamic_slice_in_dim(
         scaled_weight, lax.axis_index("rep") * local_width, local_width, 1
     )
-    moved_tokens = lax.all_to_all(tokens, "sp", split_axis=1, concat_axis=0, tiled=True)
+    moved_tokens = exchange_blocks(tokens, "sp", 1, 0)
     projected = lax.dot_general(
         moved_tokens,
         local_weight,

time: 80 us -> 80.1 us (level)
    unnamed x24 -> x23, local copies, waits for them, and re-layouts: 2.13 us -> 0.56 us
    another operation x0 -> x1, local copies, waits for them, and re-layouts: none -> 0.97 us  [exchange_blocks(): incoming = lax.all_to_all(jnp.stack(pieces), mesh_axis, 0, 0)]
where the time goes in v1:
time: 80.1 us; the launch traced here: 79.6 us
  blocking collectives  46.1 us (58%)
  starting transfers between devices  12.7 us (16%)
  waiting for transfers between devices  6.12 us (8%)
  matrix products  5.85 us (7%)
  local copies, waits for them, and re-layouts  4.64 us (6%)
  other arithmetic  3.88 us (5%)
    psum x1, blocking collectives, per_device(): lax.psum((projected, first_sums, square_sums), 'rep')  19.4 us
    psum x1, blocking collectives, per_device(): lax.psum(jnp.sum(grouped, axis=(0, 2)), ('section', 'sp')) / cell_count  14.4 us
    psum x1, blocking collectives, per_device(): lax.psum(jnp.sum(deviation * deviation, axis=(0, 2)), ('section', 'sp'))  12.2 us
    ppermute x2, starting transfers between devices, with_halo(): lax.ppermute(lax.slice_in_dim(block, block.shape[dim] - width, None, axis...  5.84 us
    conv_general_dilated x2, matrix products, valid_conv(): lax.conv_general_dilated(front[None], kernel, (1, 1, 1), 'VALID', dimensi...  4.83 us
    all_to_all x1, starting transfers between devices, exchange_blocks(): incoming = lax.all_to_all(jnp.stack(pieces), mesh_axis, 0, 0)  4.24 us
    ppermute x2, waiting for transfers between devices, with_halo(): lax.ppermute(lax.slice_in_dim(block, 0, width, axis=dim), axis, backward)  3.47 us
    ppermute x2, starting transfers between devices, with_halo(): lax.ppermute(lax.slice_in_dim(block, 0, width, axis=dim), axis, backward)  2.58 us
  transfers between devices with their start and end apart: 5, of which 3 were waited for; matrix products, arithmetic and copies ran while one was open for 4% of the time, Pallas kernels for 0%

profile of v1, /device:TPU:0, one launch (start us, length us, event | category | flops | bytes accessed | tf_op | source)
XLA Modules:
  0.0 79.6 jit_solution(3037994450119333057)
XLA Ops:
  0.0 0.0 copy-start
  0.0 0.0 copy-start.2
  0.0 1.0 %slice_bitcast_fusion.3 = (f32[1,1,1,6,768]{4,2,3,1,0:T(1,128)S(1)}, f32[1,1,1,6,768]{4,2,3,1,0:T(1,128)S(1)}) fusion(f32[1,2,6,768]{3,1,2,0:T(2,128)} %param.12), kind=kLoop, calls=%fused_computation.49 | loop fusion | bytes 73728 | tf_op jit(solution)/shard_map/stack | solution.py:14
  1.0 0.7 pad_maximum_fusion.4
  1.6 4.2 %all-to-all-start = ((f32[2,1,1,6,768]{4,2,3,1,0:T(1,128)}), f32[2,1,1,6,768]{4,2,3,1,0:T(1,128)S(1)}, u32[]{:S(2)}, u32[]{:S(2)}) async-start(f32[2,1,1,6,768]{4,2,3,1,0:T(1,128)} %pad_maximum_fusion.4), calls=%async_computation | async-start | bytes 73728 | tf_op jit(solution)/shard_map/all_to_all | solution.py:14
  5.9 0.7 broadcast_add_fusion
  6.6 1.3 %fusion.37 = (f32[64]{0:T(128)S(1)}, f32[64,3072]{1,0:T(8,128)S(1)}) fusion(f32[64,3072]{1,0:T(8,128)} %param.15, f32[3072]{0:T(1024)S(1)} %broadcast_add_fusion), kind=kLoop, calls=%fused_computation.66 | loop fusion | flops 393152 | bytes 1585408 | tf_op jit(solution)/shard_map/reduce_sum | solution.py:61
  7.9 0.0 copy-start.10
  7.9 0.0 copy-done.1
  8.0 0.7 fusion.11
  8.7 1.1 %all-to-all-done = f32[2,1,1,6,768]{4,2,3,1,0:T(1,128)S(1)} async-done(((f32[2,1,1,6,768]{4,2,3,1,0:T(1,128)}), f32[2,1,1,6,768]{4,2,3,1,0:T(1,128)S(1)}, u32[]{:S(2)}, u32[]{:S(2)}) %all-to-all-start) | async-done | bytes 36896 | tf_op jit(solution)/shard_map/all_to_all | solution.py:14
  9.9 0.3 convolution_bitcast_fusion
  10.2 0.2 multiply_reduce_fusion
  10.3 19.4 %all-reduce = (f32[2,1,6,64]{3,2,0,1:T(8,128)S(1)}, f32[2,1,6]{2,0,1:T(2,128)S(1)}, f32[2,1,6]{2,0,1:T(2,128)S(1)}) all-reduce(f32[2,1,6,64]{3,2,0,1:T(8,128)S(1)} %convolution_bitcast_fusion, f32[2,1,6]{2,0,1:T(2,128)S(1)} %bitcast.91, f32[2,1,6]{2,0,1:T(2,128)S(1)} %bitcast.90), channel_id=1, replica_groups=mesh['section'=4,'sp'=2,'rep'=4] {'rep'}, use_global_device_ids=true, to_apply=%region_4.0 | all-reduce | flops 792 | bytes 6336 | tf_op jit(solution)/shard_map/psum | solution.py:87
  29.8 0.1 add_multiply_fusion
  29.9 0.1 copy.61
  30.0 0.1 copy.62
  30.1 0.0 copy-done.2
  30.1 1.3 %collective-permute-start = (f32[2,2,2,16]{3,1,2,0:T(2,128)S(1)}, f32[2,2,2,16]{3,1,2,0:T(2,128)S(1)}, u32[]{:S(2)}, u32[]{:S(2)}) collective-permute-start(f32[2,2,2,16]{3,1,2,0:T(2,128)S(1)} %get-tuple-element.14), channel_id=1, source_target_pairs={{0,8},{8,16},{16,24},{1,9},{9,17},{17,25},{2,10},{10,18},{18,26},{... | collective-permute-start | bytes 1544 | tf_op jit(solution)/shard_map/ppermute | solution.py:23
  31.4 1.3 %collective-permute-start.1 = (f32[2,2,2,16]{3,1,2,0:T(2,128)S(1)}, f32[2,2,2,16]{3,1,2,0:T(2,128)S(1)}, u32[]{:S(2)}, u32[]{:S(2)}) collective-permute-start(f32[2,2,2,16]{3,1,2,0:T(2,128)S(1)} %get-tuple-element.15), channel_id=1, source_target_pairs={{8,0},{16,8},{24,16},{9,1},{17,9},{25,17},{10,2},{18,10},{26,18},{... | collective-permute-start | bytes 1544 | tf_op jit(solution)/shard_map/ppermute | solution.py:26
  32.8 0.0 collective-permute-done
  32.8 3.5 %collective-permute-done.1 = f32[2,2,2,16]{3,1,2,0:T(2,128)S(1)} collective-permute-done((f32[2,2,2,16]{3,1,2,0:T(2,128)S(1)}, f32[2,2,2,16]{3,1,2,0:T(2,128)S(1)}, u32[]{:S(2)}, u32[]{:S(2)}) %collective-permute-start.1) | collective-permute-done | bytes 544 | tf_op jit(solution)/shard_map/ppermute | solution.py:26
  36.3 1.3 %collective-permute-start.3 = (f32[2,2,16,16]{3,1,2,0:T(2,128)S(1)}, f32[2,2,16,16]{3,1,2,0:T(2,128)S(1)}, u32[]{:S(2)}, u32[]{:S(2)}) collective-permute-start(f32[2,2,16,16]{3,1,2,0:T(2,128)S(1)} %pad_maximum_fusion.5), channel_id=1, source_target_pairs={{4,0},{5,1},{6,2},{7,3},{12,8},{13,9},{14,10},{15,11},{20,16},{21,... | collective-permute-start | bytes 12296 | tf_op jit(solution)/shard_map/ppermute | solution.py:26
  37.6 4.5 %collective-permute-start.2 = (f32[2,2,16,16]{3,1,2,0:T(2,128)S(1)}, f32[2,2,16,16]{3,1,2,0:T(2,128)S(1)}, u32[]{:S(2)}, u32[]{:S(2)}) collective-permute-start(f32[2,2,16,16]{3,1,2,0:T(2,128)S(1)} %pad_maximum_fusion.5), channel_id=1, source_target_pairs={{0,4},{1,5},{2,6},{3,7},{8,12},{9,13},{10,14},{11,15},{16,20},{17,... | collective-permute-start | bytes 12296 | tf_op jit(solution)/shard_map/ppermute | solution.py:23
  42.1 0.1 broadcast_and_fusion
  42.2 0.0 collective-permute-done.3
  42.2 1.5 %collective-permute-done.2 = f32[2,2,16,16]{3,1,2,0:T(2,128)S(1)} collective-permute-done((f32[2,2,16,16]{3,1,2,0:T(2,128)S(1)}, f32[2,2,16,16]{3,1,2,0:T(2,128)S(1)}, u32[]{:S(2)}, u32[]{:S(2)}) %collective-permute-start.2) | collective-permute-done | bytes 4128 | tf_op jit(solution)/shard_map/ppermute | solution.py:23
  43.7 0.1 maximum_maximum_fusion
  43.9 0.0 copy-start.4
  43.9 2.8 %convolution_select_fusion = f32[2,4,8,2,512]{4,2,3,1,0:T(8,128)S(1)} fusion(f32[3,3,3,16,512]{4,3,2,1,0:T(8,128)} %param.18, f32[4,6,1,7,2,16]{5,3,4,1,0,2:T(8,128)S(1)} %slice.29, f32[4,6,1,8,2,16]{5,3,4,1,0,2:T(8,128)S(1)} %copy.65, pred[8,2]{0,1:T(4,128)(4,1)S(1)} %copy-done.10), kind=kOutput, calls=%fused_computation.8 | convolution fusion | flops 339841024 | bytes 1192976 | tf_op jit(solution)/shard_map/conv_general_dilated | solution.py:33
  46.7 0.2 copy.66
  46.9 0.1 fusion.19
  47.1 0.1 broadcast_in_dim.23
  47.2 0.1 reshape.127
  47.3 0.1 slice.31
  47.4 0.1 slice.32
  47.5 0.2 maximum_bitcast_fusion
  47.7 0.5 copy.75
  48.2 0.0 copy-start.5
  48.2 0.0 copy-start.9
  48.2 0.3 pad.1.clone
  48.5 0.4 copy.69
  48.9 0.1 slice.33
  49.0 0.0 copy-done
  49.1 0.0 copy-done.5
  49.1 0.0 copy-done.9
  49.1 0.0 copy-start.7
  49.1 0.0 copy-start.8
  49.1 2.0 %select_reduce_fusion.1 = (f32[64]{0:T(128)S(1)}, f32[2,4,8,4,64]{4,2,3,1,0:T(8,128)S(1)}) fusion(f32[64]{0:T(128)S(1)} %copy-done.5, pred[8,4]{0,1:T(4,128)(4,1)S(1)} %copy-done.9, bf16[3,3,3,64,512]{4,3,2,1,0:T(8,128)(2,1)S(1)} %copy-done, bf16[4,6,1,7,2,512]{5,3,4,1,0,2:T(8,128)(2,1)S(1)} %slice.33, bf16[4,6,1,8,4,512]{5,3,4,1,0,2:T(8,128)(2,1)S(1)} %copy.69), kind=kOutput, calls=%fused_computation.31 | convolution fusion | flops 456589248 | bytes 2966048 | tf_op jit(solution)/shard_map/conv_general_dilated | solution.py:33
  51.1 0.1 reduce_sum.69
  51.2 0.1 reduce_sum.70
  51.3 14.4 %psum.38 = f32[8]{0:T(128)S(1)} all-reduce(f32[8]{0:T(128)S(1)} %reduce_sum.70), channel_id=1, replica_groups=mesh['section'=4,'sp'=2,'rep'=4] {'section','sp'}, use_global_device_ids=true, to_apply=%region_8.9 | all-reduce | flops 8 | bytes 64 | tf_op jit(solution)/shard_map/psum | solution.py:118
  65.7 0.1 sub.42
  65.8 0.1 sub.43
  65.9 0.1 select_reduce_fusion
  66.0 0.1 reduce_sum.72
  66.1 0.1 reduce_sum.73
  66.2 12.2 %psum.39 = f32[8]{0:T(128)S(1)} all-reduce(f32[8]{0:T(128)S(1)} %reduce_sum.73), channel_id=1, replica_groups=mesh['section'=4,'sp'=2,'rep'=4] {'section','sp'}, use_global_device_ids=true, to_apply=%region_11.12 | all-reduce | flops 8 | bytes 64 | tf_op jit(solution)/shard_map/psum | solution.py:121
  78.5 0.1 mul.129
  78.6 0.1 mul.130
  78.6 0.0 copy-done.7
  78.7 0.1 multiply_bitcast_fusion
  78.7 0.2 copy.71
  78.9 0.7 copy.72
  (23 shorter events, 0.3 us)
Async XLA Ops:
  0.0 49.0 %copy-start = (bf16[3,3,3,64,512]{4,3,2,1,0:T(8,128)(2,1)S(1)}, bf16[3,3,3,64,512]{4,3,2,1,0:T(8,128)(2,1)}, u32[]{:S(2)}) copy-start(bf16[3,3,3,64,512]{4,3,2,1,0:T(8,128)(2,1)} %param.20) | copy-start | bytes 5308420
  0.0 7.9 %copy-start.1 = (f32[64,3072]{1,0:T(8,128)S(1)}, f32[64,3072]{1,0:T(8,128)}, u32[]{:S(2)}) copy-start(f32[64,3072]{1,0:T(8,128)} %param.15) | copy-start | bytes 2359300
  0.0 7.9 %copy-start.6 = (f32[64]{0:T(128)S(1)}, f32[64]{0:T(128)}, u32[]{:S(2)}) copy-start(f32[64]{0:T(128)} %param.16) | copy-start | bytes 772
  0.0 7.9 %copy-start.3 = (f32[3072]{0:T(1024)S(1)}, f32[3072]{0:T(1024)}, u32[]{:S(2)}) copy-start(f32[3072]{0:T(1024)} %param.14) | copy-start | bytes 36868
  0.0 30.1 %copy-start.2 = (f32[2,2,12,16]{3,1,2,0:T(2,128)S(1)}, f32[2,2,12,16]{3,1,2,0:T(2,128)}, u32[]{:S(2)}) copy-start(f32[2,2,12,16]{3,1,2,0:T(2,128)} %param.17) | copy-start | bytes 9220
  1.6 8.2 %all-to-all-start = ((f32[2,1,1,6,768]{4,2,3,1,0:T(1,128)}), f32[2,1,1,6,768]{4,2,3,1,0:T(1,128)S(1)}, u32[]{:S(2)}, u32[]{:S(2)}) async-start(f32[2,1,1,6,768]{4,2,3,1,0:T(1,128)} %pad_maximum_fusion.4), calls=%async_computation | async-start | bytes 73728 | tf_op jit(solution)/shard_map/all_to_all | solution.py:14
  7.9 36.0 %copy-start.10 = (pred[8,2]{0,1:T(4,128)(4,1)S(1)}, pred[8,2]{0,1:T(4,128)(4,1)}, u32[]{:S(2)}) copy-start(pred[8,2]{0,1:T(4,128)(4,1)} %constant.62) | copy-start | bytes 52
  30.1 2.6 %collective-permute-start = (f32[2,2,2,16]{3,1,2,0:T(2,128)S(1)}, f32[2,2,2,16]{3,1,2,0:T(2,128)S(1)}, u32[]{:S(2)}, u32[]{:S(2)}) collective-permute-start(f32[2,2,2,16]{3,1,2,0:T(2,128)S(1)} %get-tuple-element.14), channel_id=1, source_target_pairs={{0,8},{8,16},{16,24},{1,9},{9,17},{17,25},{2,10},{10,18},{18,26},{... | collective-permute-start | bytes 1544 | tf_op jit(solution)/shard_map/ppermute | solution.py:23
  31.4 4.8 %collective-permute-start.1 = (f32[2,2,2,16]{3,1,2,0:T(2,128)S(1)}, f32[2,2,2,16]{3,1,2,0:T(2,128)S(1)}, u32[]{:S(2)}, u32[]{:S(2)}) collective-permute-start(f32[2,2,2,16]{3,1,2,0:T(2,128)S(1)} %get-tuple-element.15), channel_id=1, source_target_pairs={{8,0},{16,8},{24,16},{9,1},{17,9},{25,17},{10,2},{18,10},{26,18},{... | collective-permute-start | bytes 1544 | tf_op jit(solution)/shard_map/ppermute | solution.py:26
  36.3 5.9 %collective-permute-start.3 = (f32[2,2,16,16]{3,1,2,0:T(2,128)S(1)}, f32[2,2,16,16]{3,1,2,0:T(2,128)S(1)}, u32[]{:S(2)}, u32[]{:S(2)}) collective-permute-start(f32[2,2,16,16]{3,1,2,0:T(2,128)S(1)} %pad_maximum_fusion.5), channel_id=1, source_target_pairs={{4,0},{5,1},{6,2},{7,3},{12,8},{13,9},{14,10},{15,11},{20,16},{21,... | collective-permute-start | bytes 12296 | tf_op jit(solution)/shard_map/ppermute | solution.py:26
  37.6 6.1 %collective-permute-start.2 = (f32[2,2,16,16]{3,1,2,0:T(2,128)S(1)}, f32[2,2,16,16]{3,1,2,0:T(2,128)S(1)}, u32[]{:S(2)}, u32[]{:S(2)}) collective-permute-start(f32[2,2,16,16]{3,1,2,0:T(2,128)S(1)} %pad_maximum_fusion.5), channel_id=1, source_target_pairs={{0,4},{1,5},{2,6},{3,7},{8,12},{9,13},{10,14},{11,15},{16,20},{17,... | collective-permute-start | bytes 12296 | tf_op jit(solution)/shard_map/ppermute | solution.py:23
  43.9 3.0 %copy-start.4 = (f32[512]{0:T(512)S(1)}, f32[512]{0:T(512)}, u32[]{:S(2)}) copy-start(f32[512]{0:T(512)} %param.19) | copy-start | bytes 6148
  48.2 0.9 %copy-start.5 = (f32[64]{0:T(128)S(1)}, f32[64]{0:T(128)}, u32[]{:S(2)}) copy-start(f32[64]{0:T(128)} %param.21) | copy-start | bytes 772
  48.2 0.9 %copy-start.9 = (pred[8,4]{0,1:T(4,128)(4,1)S(1)}, pred[8,4]{0,1:T(4,128)(4,1)}, u32[]{:S(2)}) copy-start(pred[8,4]{0,1:T(4,128)(4,1)} %constant.61) | copy-start | bytes 100
  49.1 29.6 %copy-start.7 = (f32[64]{0:T(128)S(1)}, f32[64]{0:T(128)}, u32[]{:S(2)}) copy-start(f32[64]{0:T(128)} %param.23) | copy-start | bytes 772
  49.1 29.6 %copy-start.8 = (f32[64]{0:T(128)S(1)}, f32[64]{0:T(128)}, u32[]{:S(2)}) copy-start(f32[64]{0:T(128)} %param.22) | copy-start | bytes 772
